TPU v7x, 512 devices: a whole 4x4x16 slice. The times are simulated.
512 devices in a mesh: adapter: 64 (over y, z), mp: 8 (over x, core).
Axes of the slice: x: 4, y: 4, z: 16, core: 2. Of those that a mesh axis runs over, the one named last changes fastest.
Arguments:
- tokens: bfloat16 [24576, 8192], P('adapter', 'mp'), may hold values from -6 to 6
- cotangent: bfloat16 [24576, 1024], P('adapter', 'mp'), may hold values from -6 to 6
- value_weight: bfloat16 [8192, 1024], P('mp', 'adapter'), may hold values from -0.0625 to 0.0625
- down_store: bfloat16 [128, 8, 1024, 64], P(None, 'mp', 'adapter'), may hold values from -0.0625 to 0.0625
- down_first: float32 [128, 8, 1024, 64], P(None, 'mp', 'adapter'), may hold values from -4 to 4
- down_second: float32 [128, 8, 1024, 64], P(None, 'mp', 'adapter'), may hold values from 0.01 to 1
- up_store: bfloat16 [128, 64, 1024], P(None, 'adapter', 'mp'), may hold values from -0.75 to 0.75
- up_first: float32 [128, 64, 1024], P(None, 'adapter', 'mp'), may hold values from -4 to 4
- up_second: float32 [128, 64, 1024], P(None, 'adapter', 'mp'), may hold values from 0.01 to 1
- tile_adapter: int32 [192], replicated, may hold values from 0 to 127
- tile_length: int32 [192], replicated, may hold values from 1 to 128, as said below
- adapter_slot: int32 [128], replicated, may hold values from 0 to 127, each once
Outputs:
- projected: bfloat16 [24576, 1024], P('adapter', 'mp')
- token_gradient: bfloat16 [24576, 8192], P('adapter', 'mp')
- new_down: float32 [128, 8, 1024, 64], P(None, 'mp', 'adapter')
- new_down_first: float32 [128, 8, 1024, 64], P(None, 'mp', 'adapter')
- new_down_second: float32 [128, 8, 1024, 64], P(None, 'mp', 'adapter')
- new_up: float32 [128, 64, 1024], P(None, 'adapter', 'mp')
- new_up_first: float32 [128, 64, 1024], P(None, 'adapter', 'mp')
- new_up_second: float32 [128, 64, 1024], P(None, 'adapter', 'mp')
Inputs may be any that keep to these rules, and one draw needn't show every extreme that they name: `tile_length`: some tile is full in every draw. `adapter_slot`: each slot holds exactly one adapter.
All inputs are finite; a program needn't handle non-finite values.
Results may differ from a plain program's by a relative error of at most 0.0046.
Values may be sent and summed in bfloat16 or wider, within the bound.
No kernel may reach another device: no remote copies, remote signals or barrier semaphores. Data moves between devices by JAX's collectives and lax.ppermute only.
A program may use at most 64 MiB of HBM per device.

v0:
```python
import jax
import jax.numpy as jnp
from jax import lax
from jax.sharding import Mesh, PartitionSpec as P

TILE = 128
STEP = 100
adapter_scale = 2.0
learn_rate = 0.001
beta_one = 0.9
beta_two = 0.999
adam_eps = 1e-08


def adam_step(store, first, second, gradient):
    new_first = beta_one * first + (1.0 - beta_one) * gradient
    new_second = beta_two * second + (1.0 - beta_two) * gradient * gradient
    corr_one = 1.0 - beta_one**STEP
    corr_two = 1.0 - beta_two**STEP
    moved = store.astype(jnp.float32) - learn_rate * (new_first / corr_one) / (
        jnp.sqrt(new_second / corr_two) + adam_eps
    )
    return (moved, new_first, new_second)


ADAPTER = ("ay", "az")


def gather_along(piece, axis):
    count = lax.axis_size(axis)
    got = [piece]
    for shift in range(1, count):
        pairs = [(j, (j - shift) % count) for j in range(count)]
        got.append(lax.ppermute(piece, axis, pairs))
    ordered = jnp.roll(jnp.stack(got), lax.axis_index(axis), axis=0)
    return jnp.moveaxis(ordered, 0, 1).reshape(piece.shape[0], count * piece.shape[1])


def gather_weight(value_weight):
    return gather_along(gather_along(value_weight, "az"), "ay")


def split_adapter(mesh):
    devices = mesh.devices
    n_adapter = devices.shape[0]
    try:
        n_y = len({d.coords[1] for d in devices[:, 0]})
    except (AttributeError, IndexError, TypeError):
        n_y = 1
    if n_y < 1 or n_adapter % n_y:
        n_y = 1
    return Mesh(devices.reshape(n_y, n_adapter // n_y, devices.shape[1]), ("ay", "az", "mp"))


def shards(
    tokens,
    cotangent,
    value_weight,
    down_store,
    down_first,
    down_second,
    up_store,
    up_first,
    up_second,
    tile_adapter,
    tile_length,
    adapter_slot,
):
    tile_total = tile_adapter.shape[0]
    tok_count, feat_part = tokens.shape
    head_cols = cotangent.shape[1]
    tiles_here = tok_count // TILE
    adapter_count = adapter_slot.shape[0]
    my_index = lax.axis_index(ADAPTER)
    adapter_ids = jnp.arange(adapter_count, dtype=jnp.int32)
    tile_adapter_slot = jnp.sum(
        jnp.where(tile_adapter[:, None] == adapter_ids[None, :], adapter_slot[None, :], 0), axis=1
    )
    my_lengths = lax.dynamic_slice_in_dim(tile_length, my_index * tiles_here, tiles_here)
    active_rows = (jnp.arange(TILE)[None, :] < my_lengths[:, None]).reshape(tok_count, 1)
    masked_own = cotangent * active_rows.astype(jnp.bfloat16)
    masked_full = lax.all_gather(masked_own, "mp", axis=1, tiled=True)
    n_adapter = tile_total // tiles_here
    row_part = down_store.shape[2]
    rank = down_store.shape[3]
    sent_down = down_store[:, 0][tile_adapter_slot].reshape(tile_total, row_part * rank)
    sent_up = up_store[tile_adapter_slot].reshape(tile_total, head_cols)
    sent = jnp.concatenate([sent_down, sent_up], axis=1)
    arrived = lax.all_to_all(sent, ADAPTER, split_axis=0, concat_axis=0, tiled=True)
    arrived = arrived.reshape(n_adapter, tiles_here, row_part * rank + head_cols)
    down_panel = (
        arrived[:, :, : row_part * rank]
        .reshape(n_adapter, tiles_here, row_part, rank)
        .transpose(1, 0, 2, 3)
        .reshape(tiles_here, n_adapter * row_part, rank)
    )
    up_panel = arrived[:, :, row_part * rank :].transpose(1, 0, 2)
    w_full = gather_weight(value_weight)
    token_tiles = tokens.reshape(tiles_here, TILE, feat_part)
    frozen_part = jnp.dot(tokens, w_full, preferred_element_type=jnp.float32)
    frozen_local = lax.psum_scatter(frozen_part, "mp", scatter_dimension=1, tiled=True)
    down_part = jnp.einsum(
        "ntd,ndr->ntr", token_tiles, down_panel, preferred_element_type=jnp.float32
    )
    down_sum = lax.psum(down_part, "mp")
    down_portion = down_sum.astype(jnp.bfloat16)
    adapter_term = jnp.einsum(
        "ntr,nrv->ntv", down_portion, up_panel, preferred_element_type=jnp.float32
    ).reshape(tok_count, head_cols)
    projected = (
        (frozen_local + adapter_scale * adapter_term) * active_rows.astype(jnp.float32)
    ).astype(jnp.bfloat16)
    tile_mask = masked_own.reshape(tiles_here, TILE, head_cols)
    backward_piece = adapter_scale * jnp.einsum(
        "ntv,nrv->ntr", tile_mask, up_panel, preferred_element_type=jnp.float32
    )
    backward_portion = lax.psum(backward_piece, "mp").astype(jnp.bfloat16)
    frozen_backward = lax.dot_general(
        masked_full, w_full, (((1,), (1,)), ((), ())), preferred_element_type=jnp.float32
    )
    adapter_backward = jnp.einsum(
        "ntr,ndr->ntd", backward_portion, down_panel, preferred_element_type=jnp.float32
    ).reshape(tok_count, feat_part)
    token_gradient = (frozen_backward + adapter_backward).astype(jnp.bfloat16)
    home_down = jnp.einsum(
        "ntd,ntr->ndr", token_tiles, backward_portion, preferred_element_type=jnp.float32
    )
    local_up_weight = adapter_scale * jnp.einsum(
        "ntr,ntv->nrv", down_portion, tile_mask, preferred_element_type=jnp.float32
    )
    grads = jnp.concatenate(
        [home_down.reshape(tiles_here, n_adapter, row_part * rank), local_up_weight], axis=2
    )
    grads = lax.all_to_all(grads, ADAPTER, split_axis=1, concat_axis=0, tiled=True)
    arrived_down = grads[:, 0, : row_part * rank]
    arrived_up = grads[:, 0, row_part * rank :]
    selector = (adapter_ids[:, None] == tile_adapter_slot[None, :]).astype(jnp.float32)
    down_gradient = jnp.dot(
        selector, arrived_down.reshape(tile_total, -1), precision=lax.Precision.HIGHEST
    ).reshape(down_store.shape)
    up_gradient = jnp.dot(
        selector, arrived_up.reshape(tile_total, -1), precision=lax.Precision.HIGHEST
    ).reshape(up_store.shape)
    new_down, new_down_first, new_down_second = adam_step(
        down_store, down_first, down_second, down_gradient
    )
    new_up, new_up_first, new_up_second = adam_step(up_store, up_first, up_second, up_gradient)
    return (
        projected,
        token_gradient,
        new_down,
        new_down_first,
        new_down_second,
        new_up,
        new_up_first,
        new_up_second,
    )


def solution(mesh):
    mesh = split_adapter(mesh)
    placed = (
        P(ADAPTER, "mp"),
        P(ADAPTER, "mp"),
        P("mp", ADAPTER),
        P(None, "mp", ADAPTER, None),
        P(None, "mp", ADAPTER, None),
        P(None, "mp", ADAPTER, None),
        P(None, ADAPTER, "mp"),
        P(None, ADAPTER, "mp"),
        P(None, ADAPTER, "mp"),
        P(),
        P(),
        P(),
    )
    return jax.shard_map(
        shards,
        mesh=mesh,
        in_specs=placed,
        out_specs=(
            P(ADAPTER, "mp"),
            P(ADAPTER, "mp"),
            P(None, "mp", ADAPTER, None),
            P(None, "mp", ADAPTER, None),
            P(None, "mp", ADAPTER, None),
            P(None, ADAPTER, "mp"),
            P(None, ADAPTER, "mp"),
            P(None, ADAPTER, "mp"),
        ),
        check_vma=False,
    )
```

profile of v0, /device:TPU:6, one launch (start us, length us, event | category | flops | bytes accessed | tf_op | source)
XLA Modules:
  0.0 261.7 jit_solution(3475305058610863027)
XLA Ops:
  7.2 11.5 %collective-permute-start = (bf16[1024,16]{0,1:T(8,128)(2,1)}, bf16[1024,16]{0,1:T(8,128)(2,1)S(1)}, u32[]{:S(2)}, u32[]{:S(2)}) collective-permute-start(bf16[1024,16]{0,1:T(8,128)(2,1)} %param.14), channel_id=1, source_target_pairs={{0,120},{8,0},{16,8},{24,16},{32,24},{40,32},{48,40},{56,48},{64,5... | collective-permute-start | bytes 98312 | tf_op jit(solution)/shard_map/ppermute | solution.py:34
  18.7 3.4 %collective-permute-start.1 = (bf16[1024,16]{0,1:T(8,128)(2,1)}, bf16[1024,16]{0,1:T(8,128)(2,1)S(1)}, u32[]{:S(2)}, u32[]{:S(2)}) collective-permute-start(bf16[1024,16]{0,1:T(8,128)(2,1)} %param.14), channel_id=1, source_target_pairs={{0,112},{8,120},{16,0},{24,8},{32,16},{40,24},{48,32},{56,40},{64,... | collective-permute-start | bytes 98312 | tf_op jit(solution)/shard_map/ppermute | solution.py:34
  22.1 5.0 %collective-permute-start.2 = (bf16[1024,16]{0,1:T(8,128)(2,1)}, bf16[1024,16]{0,1:T(8,128)(2,1)S(1)}, u32[]{:S(2)}, u32[]{:S(2)}) collective-permute-start(bf16[1024,16]{0,1:T(8,128)(2,1)} %param.14), channel_id=1, source_target_pairs={{0,104},{8,112},{16,120},{24,0},{32,8},{40,16},{48,24},{56,32},{64... | collective-permute-start | bytes 98312 | tf_op jit(solution)/shard_map/ppermute | solution.py:34
  27.1 2.8 %collective-permute-start.3 = (bf16[1024,16]{0,1:T(8,128)(2,1)}, bf16[1024,16]{0,1:T(8,128)(2,1)S(1)}, u32[]{:S(2)}, u32[]{:S(2)}) collective-permute-start(bf16[1024,16]{0,1:T(8,128)(2,1)} %param.14), channel_id=1, source_target_pairs={{0,96},{8,104},{16,112},{24,120},{32,0},{40,8},{48,16},{56,24},{64... | collective-permute-start | bytes 98312 | tf_op jit(solution)/shard_map/ppermute | solution.py:34
  30.0 1.9 collective-permute-start.4
  31.9 0.9 select_reduce_fusion
  32.8 1.4 copy.76
  34.2 0.8 gather_fusion
  35.0 0.5 concatenate.23
  35.5 1.5 gather_fusion.1
  37.0 1.1 pad_maximum_fusion.1
  38.1 15.8 %all-to-all-start = ((bf16[64,3,1152]{2,1,0:T(4,128)(2,1)}), bf16[64,3,1152]{2,1,0:T(4,128)(2,1)S(1)}, u32[]{:S(2)}, u32[]{:S(2)}) async-start(bf16[64,3,1152]{2,1,0:T(4,128)(2,1)} %pad_maximum_fusion.1), calls=%async_computation.1 | async-start | bytes 1179648 | tf_op jit(solution)/shard_map/all_to_all | solution.py:89
  54.0 10.4 %collective-permute-start.5 = (bf16[1024,16]{0,1:T(8,128)(2,1)S(1)}, bf16[1024,16]{0,1:T(8,128)(2,1)S(1)}, u32[]{:S(2)}, u32[]{:S(2)}) collective-permute-start(bf16[1024,16]{0,1:T(8,128)(2,1)S(1)} %copy-done.3), channel_id=1, source_target_pairs={{0,80},{8,88},{16,96},{24,104},{32,112},{40,120},{48,0},{56,8},{64... | collective-permute-start | bytes 98312 | tf_op jit(solution)/shard_map/ppermute | solution.py:34
  64.4 4.3 %collective-permute-start.6 = (bf16[1024,16]{0,1:T(8,128)(2,1)S(1)}, bf16[1024,16]{0,1:T(8,128)(2,1)S(1)}, u32[]{:S(2)}, u32[]{:S(2)}) collective-permute-start(bf16[1024,16]{0,1:T(8,128)(2,1)S(1)} %copy-done.3), channel_id=1, source_target_pairs={{0,72},{8,80},{16,88},{24,96},{32,104},{40,112},{48,120},{56,0},{6... | collective-permute-start | bytes 98312 | tf_op jit(solution)/shard_map/ppermute | solution.py:34
  68.7 9.4 %collective-permute-start.7 = (bf16[1024,16]{0,1:T(8,128)(2,1)S(1)}, bf16[1024,16]{0,1:T(8,128)(2,1)S(1)}, u32[]{:S(2)}, u32[]{:S(2)}) collective-permute-start(bf16[1024,16]{0,1:T(8,128)(2,1)S(1)} %copy-done.3), channel_id=1, source_target_pairs={{0,64},{8,72},{16,80},{24,88},{32,96},{40,104},{48,112},{56,120},{... | collective-permute-start | bytes 98312 | tf_op jit(solution)/shard_map/ppermute | solution.py:34
  78.1 3.1 %collective-permute-start.8 = (bf16[1024,16]{0,1:T(8,128)(2,1)S(1)}, bf16[1024,16]{0,1:T(8,128)(2,1)S(1)}, u32[]{:S(2)}, u32[]{:S(2)}) collective-permute-start(bf16[1024,16]{0,1:T(8,128)(2,1)S(1)} %copy-done.3), channel_id=1, source_target_pairs={{0,56},{8,64},{16,72},{24,80},{32,88},{40,96},{48,104},{56,112},{6... | collective-permute-start | bytes 98312 | tf_op jit(solution)/shard_map/ppermute | solution.py:34
  81.2 10.3 %collective-permute-start.9 = (bf16[1024,16]{0,1:T(8,128)(2,1)S(1)}, bf16[1024,16]{0,1:T(8,128)(2,1)S(1)}, u32[]{:S(2)}, u32[]{:S(2)}) collective-permute-start(bf16[1024,16]{0,1:T(8,128)(2,1)S(1)} %copy-done.3), channel_id=1, source_target_pairs={{0,48},{8,56},{16,64},{24,72},{32,80},{40,88},{48,96},{56,104},{64... | collective-permute-start | bytes 98312 | tf_op jit(solution)/shard_map/ppermute | solution.py:34
  91.5 6.7 %collective-permute-start.10 = (bf16[1024,16]{0,1:T(8,128)(2,1)S(1)}, bf16[1024,16]{0,1:T(8,128)(2,1)S(1)}, u32[]{:S(2)}, u32[]{:S(2)}) collective-permute-start(bf16[1024,16]{0,1:T(8,128)(2,1)S(1)} %copy-done.3), channel_id=1, source_target_pairs={{0,40},{8,48},{16,56},{24,64},{32,72},{40,80},{48,88},{56,96},{64,... | collective-permute-start | bytes 98312 | tf_op jit(solution)/shard_map/ppermute | solution.py:34
  98.2 1.9 collective-permute-start.11
  100.2 5.2 %collective-permute-start.12 = (bf16[1024,16]{0,1:T(8,128)(2,1)S(1)}, bf16[1024,16]{0,1:T(8,128)(2,1)S(1)}, u32[]{:S(2)}, u32[]{:S(2)}) collective-permute-start(bf16[1024,16]{0,1:T(8,128)(2,1)S(1)} %copy-done.3), channel_id=1, source_target_pairs={{0,24},{8,32},{16,40},{24,48},{32,56},{40,64},{48,72},{56,80},{64,... | collective-permute-start | bytes 98312 | tf_op jit(solution)/shard_map/ppermute | solution.py:34
  105.5 2.7 %collective-permute-start.13 = (bf16[1024,16]{0,1:T(8,128)(2,1)S(1)}, bf16[1024,16]{0,1:T(8,128)(2,1)S(1)}, u32[]{:S(2)}, u32[]{:S(2)}) collective-permute-start(bf16[1024,16]{0,1:T(8,128)(2,1)S(1)} %copy-done.3), channel_id=1, source_target_pairs={{0,16},{8,24},{16,32},{24,40},{32,48},{40,56},{48,64},{56,72},{64,... | collective-permute-start | bytes 98312 | tf_op jit(solution)/shard_map/ppermute | solution.py:34
  108.1 4.8 %collective-permute-start.14 = (bf16[1024,16]{0,1:T(8,128)(2,1)S(1)}, bf16[1024,16]{0,1:T(8,128)(2,1)S(1)}, u32[]{:S(2)}, u32[]{:S(2)}) collective-permute-start(bf16[1024,16]{0,1:T(8,128)(2,1)S(1)} %copy-done.3), channel_id=1, source_target_pairs={{0,8},{8,16},{16,24},{24,32},{32,40},{40,48},{48,56},{56,64},{64,7... | collective-permute-start | bytes 98312 | tf_op jit(solution)/shard_map/ppermute | solution.py:34
  113.4 1.8 collective-permute-done.14
  115.4 4.8 %collective-permute-start.15 = (bf16[1024,256]{0,1:T(8,128)(2,1)S(1)}, bf16[1024,256]{0,1:T(8,128)(2,1)S(1)}, u32[]{:S(2)}, u32[]{:S(2)}) collective-permute-start(bf16[1024,256]{0,1:T(8,128)(2,1)S(1)} %bitcast.143), channel_id=1, source_target_pairs={{0,384},{128,0},{256,128},{384,256},{1,385},{129,1},{257,129},{385... | collective-permute-start | bytes 1572872 | tf_op jit(solution)/shard_map/ppermute | solution.py:34
  120.3 2.5 collective-permute-start.16
  123.0 2.9 %collective-permute-start.17 = (bf16[1024,256]{0,1:T(8,128)(2,1)S(1)}, bf16[1024,256]{0,1:T(8,128)(2,1)S(1)}, u32[]{:S(2)}, u32[]{:S(2)}) collective-permute-start(bf16[1024,256]{0,1:T(8,128)(2,1)S(1)} %bitcast.145), channel_id=1, source_target_pairs={{0,128},{128,256},{256,384},{384,0},{1,129},{129,257},{257,385},{3... | collective-permute-start | bytes 1572872 | tf_op jit(solution)/shard_map/ppermute | solution.py:34
  125.9 11.5 %collective-permute-done.15 = bf16[1024,256]{0,1:T(8,128)(2,1)S(1)} collective-permute-done((bf16[1024,256]{0,1:T(8,128)(2,1)S(1)}, bf16[1024,256]{0,1:T(8,128)(2,1)S(1)}, u32[]{:S(2)}, u32[]{:S(2)}) %collective-permute-start.15) | collective-permute-done | bytes 524320 | tf_op jit(solution)/shard_map/ppermute | solution.py:34
  137.6 5.5 %collective-permute-done.17 = bf16[1024,256]{0,1:T(8,128)(2,1)S(1)} collective-permute-done((bf16[1024,256]{0,1:T(8,128)(2,1)S(1)}, bf16[1024,256]{0,1:T(8,128)(2,1)S(1)}, u32[]{:S(2)}, u32[]{:S(2)}) %collective-permute-start.17) | collective-permute-done | bytes 524320 | tf_op jit(solution)/shard_map/ppermute | solution.py:34
  143.3 1.5 constant_dynamic-slice_fusion
  146.4 22.7 %all-reduce.2 = (bf16[3,128,64]{1,2,0:T(8,128)(2,1)S(1)}, bf16[3,128,64]{1,2,0:T(8,128)(2,1)S(1)}) all-reduce(f32[3,128,64]{1,2,0:T(8,128)S(1)} %convolution_bitcast_fusion.2, f32[3,128,64]{1,2,0:T(8,128)S(1)} %convolution_multiply_fusion.2), channel_id=1, replica_groups=mesh['ay'=4,'az'=16,'mp'=8] {'mp'}, use_global_device_ids=true, to_apply=%region_2.3 | all-reduce | flops 49152 | bytes 294912 | tf_op jit(solution)/shard_map/psum | solution.py:105
  169.2 1.2 convolution_bitcast_fusion.1
  170.4 1.6 copy.82
  172.0 1.3 reshape.151
  173.3 1.2 pad_maximum_fusion
  174.5 1.6 copy.83
  176.1 10.2 %all-to-all-start.1 = ((f32[3,64,1152]{2,0,1:T(4,128)}), f32[3,64,1152]{2,0,1:T(4,128)S(1)}, u32[]{:S(2)}, u32[]{:S(2)}) async-start(f32[3,64,1152]{2,0,1:T(4,128)} %copy.83), calls=%async_computation.2 | async-start | bytes 2359296 | tf_op jit(solution)/shard_map/all_to_all | solution.py:134
  186.4 4.0 %convolution_bitcast_fusion = f32[384,1024]{0,1:T(8,128)} fusion(bf16[1024,1024]{0,1:T(8,128)(2,1)} %bitcast.150, bf16[384,1024]{1,0:T(8,128)(2,1)S(1)} %copy-done), kind=kOutput, calls=%fused_computation.4 | convolution fusion | flops 805306368 | bytes 4456448 | tf_op jit(solution)/shard_map/dot_general | solution.py:100
  190.4 15.3 %all_gather.3 = bf16[384,1024]{1,0:T(8,128)(2,1)} all-gather(bf16[384,128]{1,0:T(8,128)(2,1)S(1)} %broadcast_multiply_fusion), channel_id=1, replica_groups=mesh['ay'=4,'az'=16,'mp'=8] {'mp'}, dimensions={1}, use_global_device_ids=true | all-gather | bytes 884736 | tf_op jit(solution)/shard_map/all_gather | solution.py:82
  206.5 3.7 %fusion = bf16[384,1024]{1,0:T(8,128)(2,1)} fusion(f32[3,128,1024]{2,1,0:T(8,128)S(1)} %fusion.19, bf16[384,1024]{1,0:T(8,128)(2,1)} %all_gather.3, bf16[1024,1024]{0,1:T(8,128)(2,1)} %bitcast.151), kind=kOutput, calls=%fused_computation.3 | convolution fusion | flops 806092800 | bytes 5242880 | tf_op jit(solution)/shard_map/dot_general | solution.py:118
  210.2 19.9 %reduce-scatter.2.cloned.1.call-done = f32[384,128]{0,1:T(8,128)} async-done(((f32[384,1024]{0,1:T(8,128)}), f32[384,128]{0,1:T(8,128)}) %reduce-scatter.2.cloned.1.call-update) | async-done | bytes 196624 | tf_op jit(solution)/shard_map/reduce_scatter | solution.py:101
  230.1 1.0 multiply_convert_fusion
  231.0 0.8 copy.87
  231.8 14.7 %all-to-all-done.1 = f32[3,64,1152]{2,0,1:T(4,128)S(1)} async-done(((f32[3,64,1152]{2,0,1:T(4,128)}), f32[3,64,1152]{2,0,1:T(4,128)S(1)}, u32[]{:S(2)}, u32[]{:S(2)}) %all-to-all-start.1) | async-done | bytes 884768 | tf_op jit(solution)/shard_map/all_to_all | solution.py:134
  246.5 2.1 all_to_all.21
  248.6 1.7 slice.22
  250.3 1.0 fusion.1
  251.3 2.6 divide_subtract_fusion
  254.0 0.9 divide_subtract_fusion.1
  (93 shorter events, 3.8 us)
Async XLA Ops:
  7.2 138.8 %copy-start = (bf16[384,1024]{1,0:T(8,128)(2,1)S(1)}, bf16[384,1024]{1,0:T(8,128)(2,1)}, u32[]{:S(2)}) copy-start(bf16[384,1024]{1,0:T(8,128)(2,1)} %param.12) | copy-start | bytes 2359300
  7.2 46.7 %copy-start.3 = (bf16[1024,16]{0,1:T(8,128)(2,1)S(1)}, bf16[1024,16]{0,1:T(8,128)(2,1)}, u32[]{:S(2)}) copy-start(bf16[1024,16]{0,1:T(8,128)(2,1)} %param.14) | copy-start | bytes 98308
  7.2 46.7 %copy-start.7 = (s32[192]{0:T(256)S(1)}, s32[192]{0:T(256)}, u32[]{:S(2)}) copy-start(s32[192]{0:T(256)} %param.22) | copy-start | bytes 2308
  7.2 46.8 %collective-permute-start = (bf16[1024,16]{0,1:T(8,128)(2,1)}, bf16[1024,16]{0,1:T(8,128)(2,1)S(1)}, u32[]{:S(2)}, u32[]{:S(2)}) collective-permute-start(bf16[1024,16]{0,1:T(8,128)(2,1)} %param.14), channel_id=1, source_target_pairs={{0,120},{8,0},{16,8},{24,16},{32,24},{40,32},{48,40},{56,48},{64,5... | collective-permute-start | bytes 98312 | tf_op jit(solution)/shard_map/ppermute | solution.py:34
  18.7 45.6 %collective-permute-start.1 = (bf16[1024,16]{0,1:T(8,128)(2,1)}, bf16[1024,16]{0,1:T(8,128)(2,1)S(1)}, u32[]{:S(2)}, u32[]{:S(2)}) collective-permute-start(bf16[1024,16]{0,1:T(8,128)(2,1)} %param.14), channel_id=1, source_target_pairs={{0,112},{8,120},{16,0},{24,8},{32,16},{40,24},{48,32},{56,40},{64,... | collective-permute-start | bytes 98312 | tf_op jit(solution)/shard_map/ppermute | solution.py:34
  22.1 46.6 %collective-permute-start.2 = (bf16[1024,16]{0,1:T(8,128)(2,1)}, bf16[1024,16]{0,1:T(8,128)(2,1)S(1)}, u32[]{:S(2)}, u32[]{:S(2)}) collective-permute-start(bf16[1024,16]{0,1:T(8,128)(2,1)} %param.14), channel_id=1, source_target_pairs={{0,104},{8,112},{16,120},{24,0},{32,8},{40,16},{48,24},{56,32},{64... | collective-permute-start | bytes 98312 | tf_op jit(solution)/shard_map/ppermute | solution.py:34
  27.1 51.0 %collective-permute-start.3 = (bf16[1024,16]{0,1:T(8,128)(2,1)}, bf16[1024,16]{0,1:T(8,128)(2,1)S(1)}, u32[]{:S(2)}, u32[]{:S(2)}) collective-permute-start(bf16[1024,16]{0,1:T(8,128)(2,1)} %param.14), channel_id=1, source_target_pairs={{0,96},{8,104},{16,112},{24,120},{32,0},{40,8},{48,16},{56,24},{64... | collective-permute-start | bytes 98312 | tf_op jit(solution)/shard_map/ppermute | solution.py:34
  30.0 51.2 %collective-permute-start.4 = (bf16[1024,16]{0,1:T(8,128)(2,1)}, bf16[1024,16]{0,1:T(8,128)(2,1)S(1)}, u32[]{:S(2)}, u32[]{:S(2)}) collective-permute-start(bf16[1024,16]{0,1:T(8,128)(2,1)} %param.14), channel_id=1, source_target_pairs={{0,88},{8,96},{16,104},{24,112},{32,120},{40,0},{48,8},{56,16},{64... | collective-permute-start | bytes 98312 | tf_op jit(solution)/shard_map/ppermute | solution.py:34
  34.2 88.7 %copy-start.4 = (bf16[384,128]{1,0:T(8,128)(2,1)S(1)}, bf16[384,128]{1,0:T(8,128)(2,1)}, u32[]{:S(2)}) copy-start(bf16[384,128]{1,0:T(8,128)(2,1)} %param.13) | copy-start | bytes 294916
  38.1 106.8 %all-to-all-start = ((bf16[64,3,1152]{2,1,0:T(4,128)(2,1)}), bf16[64,3,1152]{2,1,0:T(4,128)(2,1)S(1)}, u32[]{:S(2)}, u32[]{:S(2)}) async-start(bf16[64,3,1152]{2,1,0:T(4,128)(2,1)} %pad_maximum_fusion.1), calls=%async_computation.1 | async-start | bytes 1179648 | tf_op jit(solution)/shard_map/all_to_all | solution.py:89
  54.0 37.5 %collective-permute-start.5 = (bf16[1024,16]{0,1:T(8,128)(2,1)S(1)}, bf16[1024,16]{0,1:T(8,128)(2,1)S(1)}, u32[]{:S(2)}, u32[]{:S(2)}) collective-permute-start(bf16[1024,16]{0,1:T(8,128)(2,1)S(1)} %copy-done.3), channel_id=1, source_target_pairs={{0,80},{8,88},{16,96},{24,104},{32,112},{40,120},{48,0},{56,8},{64... | collective-permute-start | bytes 98312 | tf_op jit(solution)/shard_map/ppermute | solution.py:34
  64.4 33.8 %collective-permute-start.6 = (bf16[1024,16]{0,1:T(8,128)(2,1)S(1)}, bf16[1024,16]{0,1:T(8,128)(2,1)S(1)}, u32[]{:S(2)}, u32[]{:S(2)}) collective-permute-start(bf16[1024,16]{0,1:T(8,128)(2,1)S(1)} %copy-done.3), channel_id=1, source_target_pairs={{0,72},{8,80},{16,88},{24,96},{32,104},{40,112},{48,120},{56,0},{6... | collective-permute-start | bytes 98312 | tf_op jit(solution)/shard_map/ppermute | solution.py:34
  68.7 31.5 %collective-permute-start.7 = (bf16[1024,16]{0,1:T(8,128)(2,1)S(1)}, bf16[1024,16]{0,1:T(8,128)(2,1)S(1)}, u32[]{:S(2)}, u32[]{:S(2)}) collective-permute-start(bf16[1024,16]{0,1:T(8,128)(2,1)S(1)} %copy-done.3), channel_id=1, source_target_pairs={{0,64},{8,72},{16,80},{24,88},{32,96},{40,104},{48,112},{56,120},{... | collective-permute-start | bytes 98312 | tf_op jit(solution)/shard_map/ppermute | solution.py:34
  78.1 27.3 %collective-permute-start.8 = (bf16[1024,16]{0,1:T(8,128)(2,1)S(1)}, bf16[1024,16]{0,1:T(8,128)(2,1)S(1)}, u32[]{:S(2)}, u32[]{:S(2)}) collective-permute-start(bf16[1024,16]{0,1:T(8,128)(2,1)S(1)} %copy-done.3), channel_id=1, source_target_pairs={{0,56},{8,64},{16,72},{24,80},{32,88},{40,96},{48,104},{56,112},{6... | collective-permute-start | bytes 98312 | tf_op jit(solution)/shard_map/ppermute | solution.py:34
  81.2 26.9 %collective-permute-start.9 = (bf16[1024,16]{0,1:T(8,128)(2,1)S(1)}, bf16[1024,16]{0,1:T(8,128)(2,1)S(1)}, u32[]{:S(2)}, u32[]{:S(2)}) collective-permute-start(bf16[1024,16]{0,1:T(8,128)(2,1)S(1)} %copy-done.3), channel_id=1, source_target_pairs={{0,48},{8,56},{16,64},{24,72},{32,80},{40,88},{48,96},{56,104},{64... | collective-permute-start | bytes 98312 | tf_op jit(solution)/shard_map/ppermute | solution.py:34
  91.5 21.4 %collective-permute-start.10 = (bf16[1024,16]{0,1:T(8,128)(2,1)S(1)}, bf16[1024,16]{0,1:T(8,128)(2,1)S(1)}, u32[]{:S(2)}, u32[]{:S(2)}) collective-permute-start(bf16[1024,16]{0,1:T(8,128)(2,1)S(1)} %copy-done.3), channel_id=1, source_target_pairs={{0,40},{8,48},{16,56},{24,64},{32,72},{40,80},{48,88},{56,96},{64,... | collective-permute-start | bytes 98312 | tf_op jit(solution)/shard_map/ppermute | solution.py:34
  98.2 14.7 %collective-permute-start.11 = (bf16[1024,16]{0,1:T(8,128)(2,1)S(1)}, bf16[1024,16]{0,1:T(8,128)(2,1)S(1)}, u32[]{:S(2)}, u32[]{:S(2)}) collective-permute-start(bf16[1024,16]{0,1:T(8,128)(2,1)S(1)} %copy-done.3), channel_id=1, source_target_pairs={{0,32},{8,40},{16,48},{24,56},{32,64},{40,72},{48,80},{56,88},{64,... | collective-permute-start | bytes 98312 | tf_op jit(solution)/shard_map/ppermute | solution.py:34
  100.2 12.8 %collective-permute-start.12 = (bf16[1024,16]{0,1:T(8,128)(2,1)S(1)}, bf16[1024,16]{0,1:T(8,128)(2,1)S(1)}, u32[]{:S(2)}, u32[]{:S(2)}) collective-permute-start(bf16[1024,16]{0,1:T(8,128)(2,1)S(1)} %copy-done.3), channel_id=1, source_target_pairs={{0,24},{8,32},{16,40},{24,48},{32,56},{40,64},{48,72},{56,80},{64,... | collective-permute-start | bytes 98312 | tf_op jit(solution)/shard_map/ppermute | solution.py:34
  105.5 7.9 %collective-permute-start.13 = (bf16[1024,16]{0,1:T(8,128)(2,1)S(1)}, bf16[1024,16]{0,1:T(8,128)(2,1)S(1)}, u32[]{:S(2)}, u32[]{:S(2)}) collective-permute-start(bf16[1024,16]{0,1:T(8,128)(2,1)S(1)} %copy-done.3), channel_id=1, source_target_pairs={{0,16},{8,24},{16,32},{24,40},{32,48},{40,56},{48,64},{56,72},{64,... | collective-permute-start | bytes 98312 | tf_op jit(solution)/shard_map/ppermute | solution.py:34
  108.1 7.0 %collective-permute-start.14 = (bf16[1024,16]{0,1:T(8,128)(2,1)S(1)}, bf16[1024,16]{0,1:T(8,128)(2,1)S(1)}, u32[]{:S(2)}, u32[]{:S(2)}) collective-permute-start(bf16[1024,16]{0,1:T(8,128)(2,1)S(1)} %copy-done.3), channel_id=1, source_target_pairs={{0,8},{8,16},{16,24},{24,32},{32,40},{40,48},{48,56},{56,64},{64,7... | collective-permute-start | bytes 98312 | tf_op jit(solution)/shard_map/ppermute | solution.py:34
  115.4 22.0 %collective-permute-start.15 = (bf16[1024,256]{0,1:T(8,128)(2,1)S(1)}, bf16[1024,256]{0,1:T(8,128)(2,1)S(1)}, u32[]{:S(2)}, u32[]{:S(2)}) collective-permute-start(bf16[1024,256]{0,1:T(8,128)(2,1)S(1)} %bitcast.143), channel_id=1, source_target_pairs={{0,384},{128,0},{256,128},{384,256},{1,385},{129,1},{257,129},{385... | collective-permute-start | bytes 1572872 | tf_op jit(solution)/shard_map/ppermute | solution.py:34
  120.3 17.2 %collective-permute-start.16 = (bf16[1024,256]{0,1:T(8,128)(2,1)S(1)}, bf16[1024,256]{0,1:T(8,128)(2,1)S(1)}, u32[]{:S(2)}, u32[]{:S(2)}) collective-permute-start(bf16[1024,256]{0,1:T(8,128)(2,1)S(1)} %bitcast.144), channel_id=1, source_target_pairs={{0,256},{128,384},{256,0},{384,128},{1,257},{129,385},{257,1},{385... | collective-permute-start | bytes 1572872 | tf_op jit(solution)/shard_map/ppermute | solution.py:34
  123.0 20.1 %collective-permute-start.17 = (bf16[1024,256]{0,1:T(8,128)(2,1)S(1)}, bf16[1024,256]{0,1:T(8,128)(2,1)S(1)}, u32[]{:S(2)}, u32[]{:S(2)}) collective-permute-start(bf16[1024,256]{0,1:T(8,128)(2,1)S(1)} %bitcast.145), channel_id=1, source_target_pairs={{0,128},{128,256},{256,384},{384,0},{1,129},{129,257},{257,385},{3... | collective-permute-start | bytes 1572872 | tf_op jit(solution)/shard_map/ppermute | solution.py:34
  176.1 70.4 %all-to-all-start.1 = ((f32[3,64,1152]{2,0,1:T(4,128)}), f32[3,64,1152]{2,0,1:T(4,128)S(1)}, u32[]{:S(2)}, u32[]{:S(2)}) async-start(f32[3,64,1152]{2,0,1:T(4,128)} %copy.83), calls=%async_computation.2 | async-start | bytes 2359296 | tf_op jit(solution)/shard_map/all_to_all | solution.py:134
  186.3 43.7 %reduce-scatter.2.cloned.1.call-start = ((), (), s32[]{:S(2)}) async-start(), calls=%async_computation.3 | async-start | bytes 1769472 | tf_op jit(solution)/shard_map/reduce_scatter | solution.py:101
  210.2 41.1 %copy-start.2 = (bf16[128,1,16,64]{0,3,2,1:T(8,128)(2,1)S(1)}, bf16[128,1,16,64]{0,3,2,1:T(8,128)(2,1)}, u32[]{:S(2)}) copy-start(bf16[128,1,16,64]{0,3,2,1:T(8,128)(2,1)} %param.15) | copy-start | bytes 786436
  246.5 7.4 %copy-start.1 = (bf16[128,1,128]{2,0,1:T(8,128)(2,1)S(1)}, bf16[128,1,128]{2,0,1:T(8,128)(2,1)}, u32[]{:S(2)}) copy-start(bf16[128,1,128]{2,0,1:T(8,128)(2,1)} %param.18) | copy-start | bytes 98308
  246.5 7.4 %copy-start.5 = (f32[128,1,128]{2,1,0:T(1,128)S(1)}, f32[128,1,128]{2,1,0:T(1,128)}, u32[]{:S(2)}) copy-start(f32[128,1,128]{2,1,0:T(1,128)} %param.19) | copy-start | bytes 196612
  246.5 7.4 %copy-start.6 = (f32[128,1,128]{2,1,0:T(1,128)S(1)}, f32[128,1,128]{2,1,0:T(1,128)}, u32[]{:S(2)}) copy-start(f32[128,1,128]{2,1,0:T(1,128)} %param.20) | copy-start | bytes 196612
  248.6 5.4 %slice-start = ((f32[192,1,1152]{2,1,0:T(1,128)}), f32[192,1,128]{2,1,0:T(1,128)S(1)}, s32[]{:S(2)}) async-start(f32[192,1,1152]{2,1,0:T(1,128)} %all_to_all.21), calls=%async_computation.4 | async-start | bytes 196608 | tf_op jit(solution)/shard_map/slice | solution.py:136
Sparse Core Ops, SparseCore 0:
  190.5 39.4 reduce-scatter.1
where the time goes:
time: 263 us; the launch traced here: 262 us
  starting transfers between devices  120 us (46%)
  waiting for transfers between devices  54 us (21%)
  blocking collectives  38 us (14%)
  local copies, waits for them, and re-layouts  16.4 us (6%)
  between operations  14.8 us (6%)
  matrix products  12.2 us (5%)
  other arithmetic  6.9 us (3%)
    ppermute x18, starting transfers between devices, gather_along(): got.append(lax.ppermute(piece, axis, pairs))  93.5 us
    psum x1, blocking collectives, shards(): down_sum = lax.psum(down_part, 'mp')  22.7 us
    reduce_scatter x1, waiting for transfers between devices, shards(): lax.psum_scatter(frozen_part, 'mp', scatter_dimension=1, tiled=True)  19.9 us
    ppermute x18, waiting for transfers between devices, gather_along(): got.append(lax.ppermute(piece, axis, pairs))  19.3 us
    all_to_all x1, starting transfers between devices, shards(): lax.all_to_all(sent, ADAPTER, split_axis=0, concat_axis=0, tiled=True)  15.8 us
    all_gather x1, blocking collectives, shards(): masked_full = lax.all_gather(masked_own, 'mp', axis=1, tiled=True)  15.3 us
    all_to_all x1, waiting for transfers between devices, shards(): lax.all_to_all(grads, ADAPTER, split_axis=1, concat_axis=0, tiled=True)  14.7 us
    all_to_all x1, starting transfers between devices, shards(): lax.all_to_all(grads, ADAPTER, split_axis=1, concat_axis=0, tiled=True)  10.2 us
  transfers between devices with their start and end apart: 21, of which 7 were waited for; matrix products, arithmetic and copies ran while one was open for 7% of the time, Pallas kernels for 0%

commit v1 on v0

--- a/solution.py
+++ b/solution.py
@@ -102,7 +102,7 @@
     down_part = jnp.einsum(
         "ntd,ndr->ntr", token_tiles, down_panel, preferred_element_type=jnp.float32
     )
-    down_sum = lax.psum(down_part, "mp")
+    down_sum = jnp.sum(lax.all_gather(down_part, "mp"), axis=0)
     down_portion = down_sum.astype(jnp.bfloat16)
     adapter_term = jnp.einsum(
         "ntr,nrv->ntv", down_portion, up_panel, preferred_element_type=jnp.float32

time: 263 us -> 280 us (1.065)
  blocking collectives: 38 us -> 50.8 us
    all_gather x0 -> x1, blocking collectives: none -> 15.1 us  [shards(): down_sum = jnp.sum(lax.all_gather(down_part, 'mp'), axis=0)]
where the time goes in v1:
time: 280 us; the launch traced here: 277 us
  starting transfers between devices  120 us (43%)
  waiting for transfers between devices  55 us (20%)
  blocking collectives  50.8 us (18%)
  local copies, waits for them, and re-layouts  16.3 us (6%)
  between operations  14.8 us (5%)
  matrix products  12.2 us (4%)
  other arithmetic  8.09 us (3%)
    ppermute x18, starting transfers between devices, gather_along(): got.append(lax.ppermute(piece, axis, pairs))  93.5 us
    psum x1, blocking collectives, shards(): backward_portion = lax.psum(backward_piece, 'mp').astype(jnp.bfloat16)  21.6 us
    reduce_scatter x1, waiting for transfers between devices, shards(): lax.psum_scatter(frozen_part, 'mp', scatter_dimension=1, tiled=True)  21.2 us
    ppermute x18, waiting for transfers between devices, gather_along(): got.append(lax.ppermute(piece, axis, pairs))  19.3 us
    all_to_all x1, starting transfers between devices, shards(): lax.all_to_all(sent, ADAPTER, split_axis=0, concat_axis=0, tiled=True)  15.8 us
    all_gather x1, blocking collectives, shards(): down_sum = jnp.sum(lax.all_gather(down_part, 'mp'), axis=0)  15.1 us
    all_to_all x1, waiting for transfers between devices, shards(): lax.all_to_all(grads, ADAPTER, split_axis=1, concat_axis=0, tiled=True)  14.5 us
    all_gather x1, blocking collectives, shards(): masked_full = lax.all_gather(masked_own, 'mp', axis=1, tiled=True)  14.2 us
  transfers between devices with their start and end apart: 21, of which 7 were waited for; matrix products, arithmetic and copies ran while one was open for 7% of the time, Pallas kernels for 0%

profile of v1, /device:TPU:6, one launch (start us, length us, event | category | flops | bytes accessed | tf_op | source)
XLA Modules:
  0.0 276.7 jit_solution(7047835618206040679)
XLA Ops:
  7.2 11.5 %collective-permute-start = (bf16[1024,16]{0,1:T(8,128)(2,1)}, bf16[1024,16]{0,1:T(8,128)(2,1)S(1)}, u32[]{:S(2)}, u32[]{:S(2)}) collective-permute-start(bf16[1024,16]{0,1:T(8,128)(2,1)} %param.14), channel_id=1, source_target_pairs={{0,120},{8,0},{16,8},{24,16},{32,24},{40,32},{48,40},{56,48},{64,5... | collective-permute-start | bytes 98312 | tf_op jit(solution)/shard_map/ppermute | solution.py:34
  18.7 3.4 %collective-permute-start.1 = (bf16[1024,16]{0,1:T(8,128)(2,1)}, bf16[1024,16]{0,1:T(8,128)(2,1)S(1)}, u32[]{:S(2)}, u32[]{:S(2)}) collective-permute-start(bf16[1024,16]{0,1:T(8,128)(2,1)} %param.14), channel_id=1, source_target_pairs={{0,112},{8,120},{16,0},{24,8},{32,16},{40,24},{48,32},{56,40},{64,... | collective-permute-start | bytes 98312 | tf_op jit(solution)/shard_map/ppermute | solution.py:34
  22.1 5.0 %collective-permute-start.2 = (bf16[1024,16]{0,1:T(8,128)(2,1)}, bf16[1024,16]{0,1:T(8,128)(2,1)S(1)}, u32[]{:S(2)}, u32[]{:S(2)}) collective-permute-start(bf16[1024,16]{0,1:T(8,128)(2,1)} %param.14), channel_id=1, source_target_pairs={{0,104},{8,112},{16,120},{24,0},{32,8},{40,16},{48,24},{56,32},{64... | collective-permute-start | bytes 98312 | tf_op jit(solution)/shard_map/ppermute | solution.py:34
  27.1 2.8 %collective-permute-start.3 = (bf16[1024,16]{0,1:T(8,128)(2,1)}, bf16[1024,16]{0,1:T(8,128)(2,1)S(1)}, u32[]{:S(2)}, u32[]{:S(2)}) collective-permute-start(bf16[1024,16]{0,1:T(8,128)(2,1)} %param.14), channel_id=1, source_target_pairs={{0,96},{8,104},{16,112},{24,120},{32,0},{40,8},{48,16},{56,24},{64... | collective-permute-start | bytes 98312 | tf_op jit(solution)/shard_map/ppermute | solution.py:34
  30.0 1.9 collective-permute-start.4
  31.9 0.9 select_reduce_fusion
  32.8 1.4 copy.76
  34.2 0.8 gather_fusion
  35.5 1.5 gather_fusion.1
  37.0 1.1 pad_maximum_fusion.1
  38.1 15.8 %all-to-all-start = ((bf16[64,3,1152]{2,1,0:T(4,128)(2,1)}), bf16[64,3,1152]{2,1,0:T(4,128)(2,1)S(1)}, u32[]{:S(2)}, u32[]{:S(2)}) async-start(bf16[64,3,1152]{2,1,0:T(4,128)(2,1)} %pad_maximum_fusion.1), calls=%async_computation.1 | async-start | bytes 1179648 | tf_op jit(solution)/shard_map/all_to_all | solution.py:89
  54.0 10.4 %collective-permute-start.5 = (bf16[1024,16]{0,1:T(8,128)(2,1)S(1)}, bf16[1024,16]{0,1:T(8,128)(2,1)S(1)}, u32[]{:S(2)}, u32[]{:S(2)}) collective-permute-start(bf16[1024,16]{0,1:T(8,128)(2,1)S(1)} %copy-done.3), channel_id=1, source_target_pairs={{0,80},{8,88},{16,96},{24,104},{32,112},{40,120},{48,0},{56,8},{64... | collective-permute-start | bytes 98312 | tf_op jit(solution)/shard_map/ppermute | solution.py:34
  64.4 4.3 %collective-permute-start.6 = (bf16[1024,16]{0,1:T(8,128)(2,1)S(1)}, bf16[1024,16]{0,1:T(8,128)(2,1)S(1)}, u32[]{:S(2)}, u32[]{:S(2)}) collective-permute-start(bf16[1024,16]{0,1:T(8,128)(2,1)S(1)} %copy-done.3), channel_id=1, source_target_pairs={{0,72},{8,80},{16,88},{24,96},{32,104},{40,112},{48,120},{56,0},{6... | collective-permute-start | bytes 98312 | tf_op jit(solution)/shard_map/ppermute | solution.py:34
  68.7 9.4 %collective-permute-start.7 = (bf16[1024,16]{0,1:T(8,128)(2,1)S(1)}, bf16[1024,16]{0,1:T(8,128)(2,1)S(1)}, u32[]{:S(2)}, u32[]{:S(2)}) collective-permute-start(bf16[1024,16]{0,1:T(8,128)(2,1)S(1)} %copy-done.3), channel_id=1, source_target_pairs={{0,64},{8,72},{16,80},{24,88},{32,96},{40,104},{48,112},{56,120},{... | collective-permute-start | bytes 98312 | tf_op jit(solution)/shard_map/ppermute | solution.py:34
  78.1 3.1 %collective-permute-start.8 = (bf16[1024,16]{0,1:T(8,128)(2,1)S(1)}, bf16[1024,16]{0,1:T(8,128)(2,1)S(1)}, u32[]{:S(2)}, u32[]{:S(2)}) collective-permute-start(bf16[1024,16]{0,1:T(8,128)(2,1)S(1)} %copy-done.3), channel_id=1, source_target_pairs={{0,56},{8,64},{16,72},{24,80},{32,88},{40,96},{48,104},{56,112},{6... | collective-permute-start | bytes 98312 | tf_op jit(solution)/shard_map/ppermute | solution.py:34
  81.2 10.3 %collective-permute-start.9 = (bf16[1024,16]{0,1:T(8,128)(2,1)S(1)}, bf16[1024,16]{0,1:T(8,128)(2,1)S(1)}, u32[]{:S(2)}, u32[]{:S(2)}) collective-permute-start(bf16[1024,16]{0,1:T(8,128)(2,1)S(1)} %copy-done.3), channel_id=1, source_target_pairs={{0,48},{8,56},{16,64},{24,72},{32,80},{40,88},{48,96},{56,104},{64... | collective-permute-start | bytes 98312 | tf_op jit(solution)/shard_map/ppermute | solution.py:34
  91.5 6.7 %collective-permute-start.10 = (bf16[1024,16]{0,1:T(8,128)(2,1)S(1)}, bf16[1024,16]{0,1:T(8,128)(2,1)S(1)}, u32[]{:S(2)}, u32[]{:S(2)}) collective-permute-start(bf16[1024,16]{0,1:T(8,128)(2,1)S(1)} %copy-done.3), channel_id=1, source_target_pairs={{0,40},{8,48},{16,56},{24,64},{32,72},{40,80},{48,88},{56,96},{64,... | collective-permute-start | bytes 98312 | tf_op jit(solution)/shard_map/ppermute | solution.py:34
  98.2 1.9 collective-permute-start.11
  100.2 5.2 %collective-permute-start.12 = (bf16[1024,16]{0,1:T(8,128)(2,1)S(1)}, bf16[1024,16]{0,1:T(8,128)(2,1)S(1)}, u32[]{:S(2)}, u32[]{:S(2)}) collective-permute-start(bf16[1024,16]{0,1:T(8,128)(2,1)S(1)} %copy-done.3), channel_id=1, source_target_pairs={{0,24},{8,32},{16,40},{24,48},{32,56},{40,64},{48,72},{56,80},{64,... | collective-permute-start | bytes 98312 | tf_op jit(solution)/shard_map/ppermute | solution.py:34
  105.5 2.7 collective-permute-start.13
  108.1 4.8 %collective-permute-start.14 = (bf16[1024,16]{0,1:T(8,128)(2,1)S(1)}, bf16[1024,16]{0,1:T(8,128)(2,1)S(1)}, u32[]{:S(2)}, u32[]{:S(2)}) collective-permute-start(bf16[1024,16]{0,1:T(8,128)(2,1)S(1)} %copy-done.3), channel_id=1, source_target_pairs={{0,8},{8,16},{16,24},{24,32},{32,40},{40,48},{48,56},{56,64},{64,7... | collective-permute-start | bytes 98312 | tf_op jit(solution)/shard_map/ppermute | solution.py:34
  113.4 1.8 collective-permute-done.14
  115.4 4.8 %collective-permute-start.15 = (bf16[1024,256]{0,1:T(8,128)(2,1)S(1)}, bf16[1024,256]{0,1:T(8,128)(2,1)S(1)}, u32[]{:S(2)}, u32[]{:S(2)}) collective-permute-start(bf16[1024,256]{0,1:T(8,128)(2,1)S(1)} %bitcast.144), channel_id=1, source_target_pairs={{0,384},{128,0},{256,128},{384,256},{1,385},{129,1},{257,129},{385... | collective-permute-start | bytes 1572872 | tf_op jit(solution)/shard_map/ppermute | solution.py:34
  120.3 2.5 collective-permute-start.16
  123.0 2.9 %collective-permute-start.17 = (bf16[1024,256]{0,1:T(8,128)(2,1)S(1)}, bf16[1024,256]{0,1:T(8,128)(2,1)S(1)}, u32[]{:S(2)}, u32[]{:S(2)}) collective-permute-start(bf16[1024,256]{0,1:T(8,128)(2,1)S(1)} %bitcast.146), channel_id=1, source_target_pairs={{0,128},{128,256},{256,384},{384,0},{1,129},{129,257},{257,385},{3... | collective-permute-start | bytes 1572872 | tf_op jit(solution)/shard_map/ppermute | solution.py:34
  125.9 11.5 %collective-permute-done.15 = bf16[1024,256]{0,1:T(8,128)(2,1)S(1)} collective-permute-done((bf16[1024,256]{0,1:T(8,128)(2,1)S(1)}, bf16[1024,256]{0,1:T(8,128)(2,1)S(1)}, u32[]{:S(2)}, u32[]{:S(2)}) %collective-permute-start.15) | collective-permute-done | bytes 524320 | tf_op jit(solution)/shard_map/ppermute | solution.py:34
  137.6 5.5 %collective-permute-done.17 = bf16[1024,256]{0,1:T(8,128)(2,1)S(1)} collective-permute-done((bf16[1024,256]{0,1:T(8,128)(2,1)S(1)}, bf16[1024,256]{0,1:T(8,128)(2,1)S(1)}, u32[]{:S(2)}, u32[]{:S(2)}) %collective-permute-start.17) | collective-permute-done | bytes 524320 | tf_op jit(solution)/shard_map/ppermute | solution.py:34
  143.3 1.5 constant_dynamic-slice_fusion
  145.1 21.6 %psum.7 = bf16[3,128,64]{1,2,0:T(8,128)(2,1)S(1)} all-reduce(f32[3,128,64]{1,2,0:T(8,128)S(1)} %convolution_multiply_fusion.2), channel_id=1, replica_groups=mesh['ay'=4,'az'=16,'mp'=8] {'mp'}, use_global_device_ids=true, to_apply=%region_3.4 | all-reduce | flops 24576 | bytes 147456 | tf_op jit(solution)/shard_map/psum | solution.py:117
  167.9 15.1 %all-gather = f32[24,128,64]{1,2,0:T(8,128)} all-gather(f32[3,128,64]{1,2,0:T(8,128)S(1)} %convolution_bitcast_fusion.2), channel_id=2, replica_groups=mesh['ay'=4,'az'=16,'mp'=8] {'mp'}, dimensions={0}, use_global_device_ids=true | all-gather | bytes 884736 | tf_op jit(solution)/shard_map/all_gather | solution.py:105
  183.0 1.1 convolution_bitcast_fusion.1
  184.1 1.6 copy.82
  185.8 1.3 reshape.151
  187.1 1.2 reduce_sum.22
  188.4 1.2 pad_maximum_fusion
  189.6 1.6 copy.83
  191.3 10.2 %all-to-all-start.1 = ((f32[3,64,1152]{2,0,1:T(4,128)}), f32[3,64,1152]{2,0,1:T(4,128)S(1)}, u32[]{:S(2)}, u32[]{:S(2)}) async-start(f32[3,64,1152]{2,0,1:T(4,128)} %copy.83), calls=%async_computation.2 | async-start | bytes 2359296 | tf_op jit(solution)/shard_map/all_to_all | solution.py:134
  201.5 4.0 %convolution_bitcast_fusion = f32[384,1024]{0,1:T(8,128)} fusion(bf16[1024,1024]{0,1:T(8,128)(2,1)} %bitcast.152, bf16[384,1024]{1,0:T(8,128)(2,1)S(1)} %copy-done), kind=kOutput, calls=%fused_computation.4 | convolution fusion | flops 805306368 | bytes 4456448 | tf_op jit(solution)/shard_map/dot_general | solution.py:100
  205.5 14.2 %all_gather.11 = bf16[384,1024]{1,0:T(8,128)(2,1)} all-gather(bf16[384,128]{1,0:T(8,128)(2,1)S(1)} %broadcast_multiply_fusion), channel_id=1, replica_groups=mesh['ay'=4,'az'=16,'mp'=8] {'mp'}, dimensions={1}, use_global_device_ids=true | all-gather | bytes 884736 | tf_op jit(solution)/shard_map/all_gather | solution.py:82
  220.5 3.7 %fusion = bf16[384,1024]{1,0:T(8,128)(2,1)} fusion(f32[3,128,1024]{2,1,0:T(8,128)S(1)} %fusion.19, bf16[384,1024]{1,0:T(8,128)(2,1)} %all_gather.11, bf16[1024,1024]{0,1:T(8,128)(2,1)} %bitcast.153), kind=kOutput, calls=%fused_computation.3 | convolution fusion | flops 806092800 | bytes 5242880 | tf_op jit(solution)/shard_map/dot_general | solution.py:118
  224.2 21.2 %reduce-scatter.2.cloned.1.call-done = f32[384,128]{0,1:T(8,128)} async-done(((f32[384,1024]{0,1:T(8,128)}), f32[384,128]{0,1:T(8,128)}) %reduce-scatter.2.cloned.1.call-update) | async-done | bytes 196624 | tf_op jit(solution)/shard_map/reduce_scatter | solution.py:101
  245.4 1.0 multiply_convert_fusion
  247.1 14.5 %all-to-all-done.1 = f32[3,64,1152]{2,0,1:T(4,128)S(1)} async-done(((f32[3,64,1152]{2,0,1:T(4,128)}), f32[3,64,1152]{2,0,1:T(4,128)S(1)}, u32[]{:S(2)}, u32[]{:S(2)}) %all-to-all-start.1) | async-done | bytes 884768 | tf_op jit(solution)/shard_map/all_to_all | solution.py:134
  261.5 2.0 all_to_all.21
  263.6 1.7 slice.22
  265.3 1.0 fusion.1
  266.3 2.6 divide_subtract_fusion
  269.0 0.9 divide_subtract_fusion.1
  (95 shorter events, 5.0 us)
Async XLA Ops:
  7.2 160.3 %copy-start = (bf16[384,1024]{1,0:T(8,128)(2,1)S(1)}, bf16[384,1024]{1,0:T(8,128)(2,1)}, u32[]{:S(2)}) copy-start(bf16[384,1024]{1,0:T(8,128)(2,1)} %param.12) | copy-start | bytes 2359300
  7.2 46.7 %copy-start.3 = (bf16[1024,16]{0,1:T(8,128)(2,1)S(1)}, bf16[1024,16]{0,1:T(8,128)(2,1)}, u32[]{:S(2)}) copy-start(bf16[1024,16]{0,1:T(8,128)(2,1)} %param.14) | copy-start | bytes 98308
  7.2 46.7 %copy-start.7 = (s32[192]{0:T(256)S(1)}, s32[192]{0:T(256)}, u32[]{:S(2)}) copy-start(s32[192]{0:T(256)} %param.22) | copy-start | bytes 2308
  7.2 46.8 %collective-permute-start = (bf16[1024,16]{0,1:T(8,128)(2,1)}, bf16[1024,16]{0,1:T(8,128)(2,1)S(1)}, u32[]{:S(2)}, u32[]{:S(2)}) collective-permute-start(bf16[1024,16]{0,1:T(8,128)(2,1)} %param.14), channel_id=1, source_target_pairs={{0,120},{8,0},{16,8},{24,16},{32,24},{40,32},{48,40},{56,48},{64,5... | collective-permute-start | bytes 98312 | tf_op jit(solution)/shard_map/ppermute | solution.py:34
  18.7 45.6 %collective-permute-start.1 = (bf16[1024,16]{0,1:T(8,128)(2,1)}, bf16[1024,16]{0,1:T(8,128)(2,1)S(1)}, u32[]{:S(2)}, u32[]{:S(2)}) collective-permute-start(bf16[1024,16]{0,1:T(8,128)(2,1)} %param.14), channel_id=1, source_target_pairs={{0,112},{8,120},{16,0},{24,8},{32,16},{40,24},{48,32},{56,40},{64,... | collective-permute-start | bytes 98312 | tf_op jit(solution)/shard_map/ppermute | solution.py:34
  22.1 46.6 %collective-permute-start.2 = (bf16[1024,16]{0,1:T(8,128)(2,1)}, bf16[1024,16]{0,1:T(8,128)(2,1)S(1)}, u32[]{:S(2)}, u32[]{:S(2)}) collective-permute-start(bf16[1024,16]{0,1:T(8,128)(2,1)} %param.14), channel_id=1, source_target_pairs={{0,104},{8,112},{16,120},{24,0},{32,8},{40,16},{48,24},{56,32},{64... | collective-permute-start | bytes 98312 | tf_op jit(solution)/shard_map/ppermute | solution.py:34
  27.1 51.0 %collective-permute-start.3 = (bf16[1024,16]{0,1:T(8,128)(2,1)}, bf16[1024,16]{0,1:T(8,128)(2,1)S(1)}, u32[]{:S(2)}, u32[]{:S(2)}) collective-permute-start(bf16[1024,16]{0,1:T(8,128)(2,1)} %param.14), channel_id=1, source_target_pairs={{0,96},{8,104},{16,112},{24,120},{32,0},{40,8},{48,16},{56,24},{64... | collective-permute-start | bytes 98312 | tf_op jit(solution)/shard_map/ppermute | solution.py:34
  30.0 51.2 %collective-permute-start.4 = (bf16[1024,16]{0,1:T(8,128)(2,1)}, bf16[1024,16]{0,1:T(8,128)(2,1)S(1)}, u32[]{:S(2)}, u32[]{:S(2)}) collective-permute-start(bf16[1024,16]{0,1:T(8,128)(2,1)} %param.14), channel_id=1, source_target_pairs={{0,88},{8,96},{16,104},{24,112},{32,120},{40,0},{48,8},{56,16},{64... | collective-permute-start | bytes 98312 | tf_op jit(solution)/shard_map/ppermute | solution.py:34
  34.2 88.7 %copy-start.4 = (bf16[384,128]{1,0:T(8,128)(2,1)S(1)}, bf16[384,128]{1,0:T(8,128)(2,1)}, u32[]{:S(2)}) copy-start(bf16[384,128]{1,0:T(8,128)(2,1)} %param.13) | copy-start | bytes 294916
  38.1 106.8 %all-to-all-start = ((bf16[64,3,1152]{2,1,0:T(4,128)(2,1)}), bf16[64,3,1152]{2,1,0:T(4,128)(2,1)S(1)}, u32[]{:S(2)}, u32[]{:S(2)}) async-start(bf16[64,3,1152]{2,1,0:T(4,128)(2,1)} %pad_maximum_fusion.1), calls=%async_computation.1 | async-start | bytes 1179648 | tf_op jit(solution)/shard_map/all_to_all | solution.py:89
  54.0 37.5 %collective-permute-start.5 = (bf16[1024,16]{0,1:T(8,128)(2,1)S(1)}, bf16[1024,16]{0,1:T(8,128)(2,1)S(1)}, u32[]{:S(2)}, u32[]{:S(2)}) collective-permute-start(bf16[1024,16]{0,1:T(8,128)(2,1)S(1)} %copy-done.3), channel_id=1, source_target_pairs={{0,80},{8,88},{16,96},{24,104},{32,112},{40,120},{48,0},{56,8},{64... | collective-permute-start | bytes 98312 | tf_op jit(solution)/shard_map/ppermute | solution.py:34
  64.4 33.8 %collective-permute-start.6 = (bf16[1024,16]{0,1:T(8,128)(2,1)S(1)}, bf16[1024,16]{0,1:T(8,128)(2,1)S(1)}, u32[]{:S(2)}, u32[]{:S(2)}) collective-permute-start(bf16[1024,16]{0,1:T(8,128)(2,1)S(1)} %copy-done.3), channel_id=1, source_target_pairs={{0,72},{8,80},{16,88},{24,96},{32,104},{40,112},{48,120},{56,0},{6... | collective-permute-start | bytes 98312 | tf_op jit(solution)/shard_map/ppermute | solution.py:34
  68.7 31.5 %collective-permute-start.7 = (bf16[1024,16]{0,1:T(8,128)(2,1)S(1)}, bf16[1024,16]{0,1:T(8,128)(2,1)S(1)}, u32[]{:S(2)}, u32[]{:S(2)}) collective-permute-start(bf16[1024,16]{0,1:T(8,128)(2,1)S(1)} %copy-done.3), channel_id=1, source_target_pairs={{0,64},{8,72},{16,80},{24,88},{32,96},{40,104},{48,112},{56,120},{... | collective-permute-start | bytes 98312 | tf_op jit(solution)/shard_map/ppermute | solution.py:34
  78.1 27.3 %collective-permute-start.8 = (bf16[1024,16]{0,1:T(8,128)(2,1)S(1)}, bf16[1024,16]{0,1:T(8,128)(2,1)S(1)}, u32[]{:S(2)}, u32[]{:S(2)}) collective-permute-start(bf16[1024,16]{0,1:T(8,128)(2,1)S(1)} %copy-done.3), channel_id=1, source_target_pairs={{0,56},{8,64},{16,72},{24,80},{32,88},{40,96},{48,104},{56,112},{6... | collective-permute-start | bytes 98312 | tf_op jit(solution)/shard_map/ppermute | solution.py:34
  81.2 26.9 %collective-permute-start.9 = (bf16[1024,16]{0,1:T(8,128)(2,1)S(1)}, bf16[1024,16]{0,1:T(8,128)(2,1)S(1)}, u32[]{:S(2)}, u32[]{:S(2)}) collective-permute-start(bf16[1024,16]{0,1:T(8,128)(2,1)S(1)} %copy-done.3), channel_id=1, source_target_pairs={{0,48},{8,56},{16,64},{24,72},{32,80},{40,88},{48,96},{56,104},{64... | collective-permute-start | bytes 98312 | tf_op jit(solution)/shard_map/ppermute | solution.py:34
  91.5 21.4 %collective-permute-start.10 = (bf16[1024,16]{0,1:T(8,128)(2,1)S(1)}, bf16[1024,16]{0,1:T(8,128)(2,1)S(1)}, u32[]{:S(2)}, u32[]{:S(2)}) collective-permute-start(bf16[1024,16]{0,1:T(8,128)(2,1)S(1)} %copy-done.3), channel_id=1, source_target_pairs={{0,40},{8,48},{16,56},{24,64},{32,72},{40,80},{48,88},{56,96},{64,... | collective-permute-start | bytes 98312 | tf_op jit(solution)/shard_map/ppermute | solution.py:34
  98.2 14.7 %collective-permute-start.11 = (bf16[1024,16]{0,1:T(8,128)(2,1)S(1)}, bf16[1024,16]{0,1:T(8,128)(2,1)S(1)}, u32[]{:S(2)}, u32[]{:S(2)}) collective-permute-start(bf16[1024,16]{0,1:T(8,128)(2,1)S(1)} %copy-done.3), channel_id=1, source_target_pairs={{0,32},{8,40},{16,48},{24,56},{32,64},{40,72},{48,80},{56,88},{64,... | collective-permute-start | bytes 98312 | tf_op jit(solution)/shard_map/ppermute | solution.py:34
  100.2 12.8 %collective-permute-start.12 = (bf16[1024,16]{0,1:T(8,128)(2,1)S(1)}, bf16[1024,16]{0,1:T(8,128)(2,1)S(1)}, u32[]{:S(2)}, u32[]{:S(2)}) collective-permute-start(bf16[1024,16]{0,1:T(8,128)(2,1)S(1)} %copy-done.3), channel_id=1, source_target_pairs={{0,24},{8,32},{16,40},{24,48},{32,56},{40,64},{48,72},{56,80},{64,... | collective-permute-start | bytes 98312 | tf_op jit(solution)/shard_map/ppermute | solution.py:34
  105.5 7.9 %collective-permute-start.13 = (bf16[1024,16]{0,1:T(8,128)(2,1)S(1)}, bf16[1024,16]{0,1:T(8,128)(2,1)S(1)}, u32[]{:S(2)}, u32[]{:S(2)}) collective-permute-start(bf16[1024,16]{0,1:T(8,128)(2,1)S(1)} %copy-done.3), channel_id=1, source_target_pairs={{0,16},{8,24},{16,32},{24,40},{32,48},{40,56},{48,64},{56,72},{64,... | collective-permute-start | bytes 98312 | tf_op jit(solution)/shard_map/ppermute | solution.py:34
  108.1 7.0 %collective-permute-start.14 = (bf16[1024,16]{0,1:T(8,128)(2,1)S(1)}, bf16[1024,16]{0,1:T(8,128)(2,1)S(1)}, u32[]{:S(2)}, u32[]{:S(2)}) collective-permute-start(bf16[1024,16]{0,1:T(8,128)(2,1)S(1)} %copy-done.3), channel_id=1, source_target_pairs={{0,8},{8,16},{16,24},{24,32},{32,40},{40,48},{48,56},{56,64},{64,7... | collective-permute-start | bytes 98312 | tf_op jit(solution)/shard_map/ppermute | solution.py:34
  115.4 22.0 %collective-permute-start.15 = (bf16[1024,256]{0,1:T(8,128)(2,1)S(1)}, bf16[1024,256]{0,1:T(8,128)(2,1)S(1)}, u32[]{:S(2)}, u32[]{:S(2)}) collective-permute-start(bf16[1024,256]{0,1:T(8,128)(2,1)S(1)} %bitcast.144), channel_id=1, source_target_pairs={{0,384},{128,0},{256,128},{384,256},{1,385},{129,1},{257,129},{385... | collective-permute-start | bytes 1572872 | tf_op jit(solution)/shard_map/ppermute | solution.py:34
  120.3 17.2 %collective-permute-start.16 = (bf16[1024,256]{0,1:T(8,128)(2,1)S(1)}, bf16[1024,256]{0,1:T(8,128)(2,1)S(1)}, u32[]{:S(2)}, u32[]{:S(2)}) collective-permute-start(bf16[1024,256]{0,1:T(8,128)(2,1)S(1)} %bitcast.145), channel_id=1, source_target_pairs={{0,256},{128,384},{256,0},{384,128},{1,257},{129,385},{257,1},{385... | collective-permute-start | bytes 1572872 | tf_op jit(solution)/shard_map/ppermute | solution.py:34
  123.0 20.1 %collective-permute-start.17 = (bf16[1024,256]{0,1:T(8,128)(2,1)S(1)}, bf16[1024,256]{0,1:T(8,128)(2,1)S(1)}, u32[]{:S(2)}, u32[]{:S(2)}) collective-permute-start(bf16[1024,256]{0,1:T(8,128)(2,1)S(1)} %bitcast.146), channel_id=1, source_target_pairs={{0,128},{128,256},{256,384},{384,0},{1,129},{129,257},{257,385},{3... | collective-permute-start | bytes 1572872 | tf_op jit(solution)/shard_map/ppermute | solution.py:34
  191.3 70.3 %all-to-all-start.1 = ((f32[3,64,1152]{2,0,1:T(4,128)}), f32[3,64,1152]{2,0,1:T(4,128)S(1)}, u32[]{:S(2)}, u32[]{:S(2)}) async-start(f32[3,64,1152]{2,0,1:T(4,128)} %copy.83), calls=%async_computation.2 | async-start | bytes 2359296 | tf_op jit(solution)/shard_map/all_to_all | solution.py:134
  201.5 43.9 %reduce-scatter.2.cloned.1.call-start = ((), (), s32[]{:S(2)}) async-start(), calls=%async_computation.3 | async-start | bytes 1769472 | tf_op jit(solution)/shard_map/reduce_scatter | solution.py:101
  224.2 42.1 %copy-start.2 = (bf16[128,1,16,64]{0,3,2,1:T(8,128)(2,1)S(1)}, bf16[128,1,16,64]{0,3,2,1:T(8,128)(2,1)}, u32[]{:S(2)}) copy-start(bf16[128,1,16,64]{0,3,2,1:T(8,128)(2,1)} %param.15) | copy-start | bytes 786436
  261.5 7.4 %copy-start.1 = (bf16[128,1,128]{2,0,1:T(8,128)(2,1)S(1)}, bf16[128,1,128]{2,0,1:T(8,128)(2,1)}, u32[]{:S(2)}) copy-start(bf16[128,1,128]{2,0,1:T(8,128)(2,1)} %param.18) | copy-start | bytes 98308
  261.5 7.4 %copy-start.5 = (f32[128,1,128]{2,1,0:T(1,128)S(1)}, f32[128,1,128]{2,1,0:T(1,128)}, u32[]{:S(2)}) copy-start(f32[128,1,128]{2,1,0:T(1,128)} %param.19) | copy-start | bytes 196612
  261.5 7.4 %copy-start.6 = (f32[128,1,128]{2,1,0:T(1,128)S(1)}, f32[128,1,128]{2,1,0:T(1,128)}, u32[]{:S(2)}) copy-start(f32[128,1,128]{2,1,0:T(1,128)} %param.20) | copy-start | bytes 196612
  263.6 5.4 %slice-start = ((f32[192,1,1152]{2,1,0:T(1,128)}), f32[192,1,128]{2,1,0:T(1,128)S(1)}, s32[]{:S(2)}) async-start(f32[192,1,1152]{2,1,0:T(1,128)} %all_to_all.21), calls=%async_computation.4 | async-start | bytes 196608 | tf_op jit(solution)/shard_map/slice | solution.py:136
Sparse Core Ops, SparseCore 0:
  205.7 39.6 reduce-scatter.1
